TPU v7x, 512 devices: a whole 4x8x8 slice. The times are simulated.
512 devices in a mesh: req: 64 (over x, y, core), tp: 8 (over z).
Axes of the slice: x: 4, y: 8, z: 8, core: 2. Of those that a mesh axis runs over, the one named last changes fastest.
Arguments:
- vit_context: bfloat16 [32768, 4096], P('req', 'tp'), may hold values from -6 to 6
- vision_residual: bfloat16 [32768, 4096], P('req', 'tp'), may hold values from -75 to 75
- out_weight: bfloat16 [4096, 4096], P('tp', 'req'), may hold values from -0.09375 to 0.09375
- layer_scale: float32 [4096], P('tp'), may hold values from 0.2 to 2
- prompt: bfloat16 [64, 256, 4096], P('req', None, 'tp'), may hold values from -75 to 75
- prompt_len: int32 [64], P('req'), may hold values from 128 to 256
- image_at: int32 [64], P('req'), may hold values from 0 to 128
- grid_sizes: int32 [128, 2], replicated, may hold values from 7 to 8, as said below
- image_owner: int32 [128], replicated, may hold values from 0 to 63, as said below
- norm_gain: float32 [4096], replicated, may hold values from 0.5 to 1.5
- qkv_weight: bfloat16 [4096, 6144], P('req', 'tp'), may hold values from -0.09375 to 0.09375
Outputs:
- qkv: bfloat16 [24576, 6144], P('req', 'tp')
Inputs may be any that keep to these rules, and one draw needn't show every extreme that they name: `image_owner`: each request owns exactly 2 images. `grid_sizes`: each side is 7 or 8; in every draw the images of some request are all 8 by 8, so that request has exactly 128 merged rows.
All inputs are finite; a program needn't handle non-finite values.
Results may differ from a plain program's by a relative error of at most 0.008.
Values may be sent and summed in bfloat16 or wider, within the bound.
No kernel may reach another device: no remote copies, remote signals or barrier semaphores. Data moves between devices by JAX's collectives and lax.ppermute only.
A program may use at most 64 MiB of HBM per device.

v0:
```python
import jax
import jax.numpy as jnp
from jax import lax
from jax.sharding import PartitionSpec as P

HEAD = 128
GROUP = 4
IMG_MAX = 128


def request_plan(grid_sizes, image_owner, requests):
    image_rows = grid_sizes[:, 0] * grid_sizes[:, 1]
    member = (image_owner[:, None] == jnp.arange(requests, dtype=jnp.int32)[None, :]).astype(
        jnp.int32
    )
    counts = jnp.sum(image_rows[:, None] * member, axis=0)
    starts = jnp.cumsum(counts) - counts
    return (counts, starts)


def rope_tables(count):
    half_size = HEAD // 2
    exponent = jnp.arange(half_size, dtype=jnp.float32) * (2.0 / HEAD)
    frequency = jnp.exp(-exponent * jnp.log(jnp.float32(500000.0)))
    angles = jnp.arange(count, dtype=jnp.float32)[:, None] * frequency[None, :]
    return (jnp.cos(angles), jnp.sin(angles))


def apply_rope(projected, cosine_table, sine_table):
    seq_rows = projected.shape[0]
    head_blocks = projected.reshape(seq_rows, -1, GROUP + 2, HEAD)
    turning = head_blocks[:, :, : GROUP + 1, :]
    first_half = turning[..., : HEAD // 2]
    second_half = turning[..., HEAD // 2 :]
    cosine_wide = cosine_table[:, None, None, :]
    sine_wide = sine_table[:, None, None, :]
    turned = jnp.concatenate(
        [
            first_half * cosine_wide - second_half * sine_wide,
            second_half * cosine_wide + first_half * sine_wide,
        ],
        axis=-1,
    )
    head_blocks = jnp.concatenate([turned, head_blocks[:, :, GROUP + 1 :, :]], axis=2)
    return head_blocks.reshape(seq_rows, -1)


def normalize(embedded, norm_gain):
    values = embedded.astype(jnp.float32)
    mean_square = jnp.mean(values * values, axis=-1, keepdims=True)
    return (values * lax.rsqrt(mean_square + 1e-05) * norm_gain[None, :]).astype(jnp.bfloat16)


def shards(
    vit_context,
    vision_residual,
    out_weight,
    layer_scale,
    prompt,
    prompt_len,
    image_at,
    grid_sizes,
    image_owner,
    norm_gain,
    qkv_weight,
):
    requests = lax.axis_size("req")
    device_index = lax.axis_index("req")
    feature_width = vit_context.shape[1]
    merged_context = jnp.mean(
        vit_context.astype(jnp.float32).reshape(-1, 4, feature_width), axis=1
    ).astype(jnp.bfloat16)
    merged_residual = jnp.mean(
        vision_residual.astype(jnp.float32).reshape(-1, 4, feature_width), axis=1
    )
    partial_value = jnp.dot(
        merged_context,
        lax.all_gather(out_weight, "req", axis=1, tiled=True),
        preferred_element_type=jnp.float32,
    )
    summed = lax.psum(partial_value.astype(jnp.bfloat16), "tp").astype(jnp.float32)
    own_share = lax.dynamic_slice_in_dim(
        summed, lax.axis_index("tp") * feature_width, feature_width, 1
    )
    merged = (merged_residual + layer_scale[None, :] * own_share).astype(jnp.bfloat16)
    merged_count = merged.shape[0]
    counts, starts = request_plan(grid_sizes, image_owner, requests)
    request_ends = starts + counts
    capacity = (IMG_MAX + requests - 1) // requests
    request_ids = jnp.arange(requests, dtype=jnp.int32)
    group_index = jnp.arange(merged_count, dtype=jnp.int32) * requests + device_index
    destination = jnp.sum((request_ends[None, :] <= group_index[:, None]).astype(jnp.int32), axis=1)
    owned_start = jnp.sum(
        jnp.where(destination[:, None] == request_ids[None, :], starts[None, :], 0), axis=1
    )
    target = destination * capacity + (group_index - owned_start) // requests
    usable = destination < requests
    send_slots = jnp.arange(requests * capacity, dtype=jnp.int32)
    placing = ((send_slots[:, None] == target[None, :]) & usable[None, :]).astype(jnp.bfloat16)
    outgoing = jnp.dot(placing, merged, preferred_element_type=jnp.float32).astype(jnp.bfloat16)
    arrived = lax.all_to_all(
        outgoing.reshape(requests, capacity, feature_width),
        "req",
        split_axis=0,
        concat_axis=0,
        tiled=True,
    )
    arrived = arrived.reshape(requests * capacity, feature_width)
    own_request = request_ids == device_index
    own_count = jnp.sum(jnp.where(own_request, counts, 0))
    own_start = jnp.sum(jnp.where(own_request, starts, 0))
    image_from = image_at[0]
    prompt_count = prompt_len[0]
    seq_slots = prompt.shape[1] + IMG_MAX
    slot_index = jnp.arange(seq_slots, dtype=jnp.int32)
    image_row = slot_index - image_from
    in_image = (image_row >= 0) & (image_row < own_count)
    is_live = slot_index < prompt_count + own_count
    from_prompt = is_live & jnp.logical_not(in_image)
    flat_index = (own_start + image_row) % requests * capacity + image_row // requests
    image_pick = ((flat_index[:, None] == send_slots[None, :]) & in_image[:, None]).astype(
        jnp.bfloat16
    )
    prompt_row = jnp.where(slot_index < image_from, slot_index, slot_index - own_count)
    prompt_ids = jnp.arange(prompt.shape[1], dtype=jnp.int32)
    prompt_pick = ((prompt_row[:, None] == prompt_ids[None, :]) & from_prompt[:, None]).astype(
        jnp.bfloat16
    )
    embedded = (
        jnp.dot(image_pick, arrived, preferred_element_type=jnp.float32)
        + jnp.dot(prompt_pick, prompt[0], preferred_element_type=jnp.float32)
    ).astype(jnp.bfloat16)
    gathered = lax.all_gather(embedded, "tp", axis=1, tiled=True)
    normed = normalize(gathered, norm_gain)
    projected = jnp.dot(
        normed,
        lax.all_gather(qkv_weight, "req", axis=0, tiled=True),
        preferred_element_type=jnp.float32,
    )
    cosine_table, sine_table = rope_tables(seq_slots)
    return apply_rope(projected, cosine_table, sine_table).astype(jnp.bfloat16)


def solution(mesh):
    in_specs = (
        P("req", "tp"),
        P("req", "tp"),
        P("tp", "req"),
        P("tp"),
        P("req", None, "tp"),
        P("req"),
        P("req"),
        P(),
        P(),
        P(),
        P("req", "tp"),
    )
    out_specs = P("req", "tp")
    return jax.shard_map(shards, mesh=mesh, in_specs=in_specs, out_specs=out_specs, check_vma=False)
```

profile of v0, /device:TPU:1, one launch (start us, length us, event | category | flops | bytes accessed | tf_op | source)
XLA Modules:
  0.0 352.9 jit_solution(7770393168710454331)
XLA Ops:
  6.5 0.0 copy-start
  6.5 0.0 all-gather.4.cloned.1.call-start
  6.5 0.7 all-gather.4.cloned.1.call-update
  7.3 0.0 all-reduce.2.cloned.1.call-start
  7.3 1.4 reshape.205
  8.7 0.0 copy-start.4
  8.7 0.0 copy-start.1
  8.7 0.6 reduce_sum.78
  9.3 0.8 multiply_bitcast_fusion
  10.1 91.0 %all-gather.4.cloned.1.call-done = bf16[512,4096]{0,1:T(8,128)(2,1)} async-done(((bf16[512,64]{0,1:T(8,128)(2,1)}), bf16[512,4096]{0,1:T(8,128)(2,1)}) %all-gather.4.cloned.1.call-update) | async-done | bytes 4194320 | tf_op jit(solution)/shard_map/all_gather | solution.py:78
  101.1 4.6 %convolution_convert_fusion = bf16[128,4096]{1,0:T(8,128)(2,1)} fusion(bf16[512,4096]{0,1:T(8,128)(2,1)} %all-gather.4.cloned.1.call-done, f32[128,512]{1,0:T(8,128)S(1)} %reduce_sum.78), kind=kOutput, calls=%fused_computation.5 | convolution fusion | flops 537526272 | bytes 5505024 | tf_op jit(solution)/shard_map/dot_general | solution.py:76
  105.7 0.0 all-reduce.2.cloned.1.call-update
  105.7 0.0 copy-done.4
  105.7 0.1 select_reduce_fusion.1
  105.8 0.1 copy.16
  105.9 0.1 reduce-window.7
  106.0 0.1 reduce
  106.2 0.0 copy-done.1
  106.2 0.3 reshape.203
  106.5 0.0 copy-start.3
  106.5 0.6 reduce_sum.77
  107.2 0.1 convert_reduce_fusion
  107.3 0.7 fusion.38
  108.0 0.1 select_reduce_fusion
  108.1 73.3 %all-reduce.2.cloned.1.call-done = bf16[128,4096]{1,0:T(8,128)(2,1)} async-done(((bf16[128,4096]{1,0:T(8,128)(2,1)}), bf16[128,4096]{1,0:T(8,128)(2,1)}) %all-reduce.2.cloned.1.call-update) | async-done | bytes 1048592 | tf_op jit(solution)/shard_map/psum | solution.py:81
  181.4 0.0 copy-done.2
  181.4 1.1 convolution_convert_fusion.1
  182.5 0.7 reshape.199
  183.3 14.2 %all-to-all-start = ((bf16[64,2,512]{2,1,0:T(2,128)(2,1)}), bf16[64,2,512]{2,1,0:T(2,128)(2,1)S(1)}, u32[]{:S(2)}, u32[]{:S(2)}) async-start(bf16[64,2,512]{2,1,0:T(2,128)(2,1)} %reshape.199), calls=%async_computation | async-start | bytes 262144 | tf_op jit(solution)/shard_map/all_to_all | solution.py:101
  197.4 0.0 all-gather.6.cloned.1.call-start
  199.3 0.6 fusion.37
  199.9 1.3 fusion.30
  201.2 6.6 %all-to-all-done = bf16[64,2,512]{2,1,0:T(2,128)(2,1)S(1)} async-done(((bf16[64,2,512]{2,1,0:T(2,128)(2,1)}), bf16[64,2,512]{2,1,0:T(2,128)(2,1)S(1)}, u32[]{:S(2)}, u32[]{:S(2)}) %all-to-all-start) | async-done | bytes 131104 | tf_op jit(solution)/shard_map/all_to_all | solution.py:101
  207.8 0.1 reshape.200
  207.9 0.3 fusion.14
  208.2 0.0 copy-done
  208.2 1.1 fusion.7
  209.3 0.0 all-gather.6.cloned.1.call-update
  209.3 0.0 all-gather.8.cloned.1.call-start
  209.3 0.5 all-gather.8.cloned.1.call-update
  209.9 0.4 fusion.21
  210.3 40.0 %all-gather.6.cloned.1.call-done = bf16[384,4096]{1,0:T(8,128)(2,1)} async-done(((bf16[384,512]{1,0:T(8,128)(2,1)}), bf16[384,4096]{1,0:T(8,128)(2,1)}) %all-gather.6.cloned.1.call-update) | async-done | bytes 3145744 | tf_op jit(solution)/shard_map/all_gather | solution.py:133
  250.3 2.6 fusion
  252.9 85.4 %all-gather.8.cloned.1.call-done = bf16[4096,768]{1,0:T(8,128)(2,1)} async-done(((bf16[64,768]{1,0:T(8,128)(2,1)}), bf16[4096,768]{1,0:T(8,128)(2,1)}) %all-gather.8.cloned.1.call-update) | async-done | bytes 6291472 | tf_op jit(solution)/shard_map/all_gather | solution.py:137
  338.3 6.7 %fusion.3 = f32[384,768]{0,1:T(8,128)S(1)} fusion(bf16[4096,768]{1,0:T(8,128)(2,1)} %all-gather.8.cloned.1.call-done, bf16[384,4096]{1,0:T(8,128)(2,1)} %all-gather.6.cloned.1.call-done, f32[4096]{0:T(1024)S(1)} %copy-done.3, f32[384]{0:T(512)S(1)} %add_rsqrt_fusion), kind=kOutput, calls=%fused_computation.6 | convolution fusion | flops 2422210560 | bytes 10634752 | tf_op jit(solution)/shard_map/dot_general | solution.py:135
  345.0 0.1 subtract_convert_fusion
  345.2 0.1 pad_maximum_fusion
  345.2 1.1 copy.18
  (8 shorter events, 0.1 us)
Async XLA Ops:
  6.5 201.7 %copy-start = (bf16[1,256,512]{2,1,0:T(8,128)(2,1)S(1)}, bf16[1,256,512]{2,1,0:T(8,128)(2,1)}, u32[]{:S(2)}) copy-start(bf16[1,256,512]{2,1,0:T(8,128)(2,1)} %param.15) | copy-start | bytes 786436
  6.5 94.5 %all-gather.4.cloned.1.call-start = ((), (), s32[]{:S(2)}) async-start(), calls=%async_computation.1 | async-start | bytes 4259840 | tf_op jit(solution)/shard_map/all_gather | solution.py:78
  7.3 174.2 %all-reduce.2.cloned.1.call-start = ((), (), s32[]{:S(2)}) async-start(), calls=%async_computation.2 | async-start | bytes 2097152 | tf_op jit(solution)/shard_map/psum | solution.py:81
  8.7 97.0 %copy-start.4 = (s32[128]{0:T(128)S(1)}, s32[128]{0:T(128)}, u32[]{:S(2)}) copy-start(s32[128]{0:T(128)} %param.19) | copy-start | bytes 1540
  8.7 97.5 %copy-start.1 = (bf16[512,512]{1,0:T(8,128)(2,1)S(1)}, bf16[512,512]{1,0:T(8,128)(2,1)}, u32[]{:S(2)}) copy-start(bf16[512,512]{1,0:T(8,128)(2,1)} %param.12) | copy-start | bytes 1572868
  10.1 171.3 %copy-start.2 = (f32[512]{0:T(512)S(1)}, f32[512]{0:T(512)}, u32[]{:S(2)}) copy-start(f32[512]{0:T(512)} %param.14) | copy-start | bytes 6148
  106.5 231.8 %copy-start.3 = (f32[4096]{0:T(1024)S(1)}, f32[4096]{0:T(1024)}, u32[]{:S(2)}) copy-start(f32[4096]{0:T(1024)} %param.20) | copy-start | bytes 49156
  183.3 24.5 %all-to-all-start = ((bf16[64,2,512]{2,1,0:T(2,128)(2,1)}), bf16[64,2,512]{2,1,0:T(2,128)(2,1)S(1)}, u32[]{:S(2)}, u32[]{:S(2)}) async-start(bf16[64,2,512]{2,1,0:T(2,128)(2,1)} %reshape.199), calls=%async_computation | async-start | bytes 262144 | tf_op jit(solution)/shard_map/all_to_all | solution.py:101
  197.4 52.9 %all-gather.6.cloned.1.call-start = ((), (), s32[]{:S(2)}) async-start(), calls=%async_computation.3 | async-start | bytes 3538944 | tf_op jit(solution)/shard_map/all_gather | solution.py:133
  209.3 129.0 %all-gather.8.cloned.1.call-start = ((), (), s32[]{:S(2)}) async-start(), calls=%async_computation.4 | async-start | bytes 6389760 | tf_op jit(solution)/shard_map/all_gather | solution.py:137
Sparse Core Ops, SparseCore 0:
  10.7 90.2 all-gather.3
  105.8 75.5 all-reduce.1
  209.4 40.8 all-gather.5
  253.5 84.7 all-gather.7
where the time goes:
time: 353 us
  waiting for transfers between devices  298 us (84%)
  between operations  15.2 us (4%)
  starting transfers between devices  14.3 us (4%)
  matrix products  13.8 us (4%)
  other arithmetic  8.27 us (2%)
  local copies, waits for them, and re-layouts  3.69 us (1%)
    all_gather x1, waiting for transfers between devices, shards(): lax.all_gather(out_weight, 'req', axis=1, tiled=True)  91 us
    all_gather x1, waiting for transfers between devices, shards(): lax.all_gather(qkv_weight, 'req', axis=0, tiled=True)  85.4 us
    psum x1, waiting for transfers between devices, shards(): lax.psum(partial_value.astype(jnp.bfloat16), 'tp').astype(jnp.float32)  73.3 us
    all_gather x1, waiting for transfers between devices, shards(): gathered = lax.all_gather(embedded, 'tp', axis=1, tiled=True)  40 us
    all_to_all x1, starting transfers between devices, shards(): lax.all_to_all(outgoing.reshape(requests, capacity, feature_width), 'req'...  14.2 us
  transfers between devices with their start and end apart: 5, of which 5 were waited for; matrix products, arithmetic and copies ran while one was open for 3% of the time, Pallas kernels for 0%

commit v1 on v0

--- a/solution.py
+++ b/solution.py
@@ -130,7 +130,12 @@
         jnp.dot(image_pick, arrived, preferred_element_type=jnp.float32)
         + jnp.dot(prompt_pick, prompt[0], preferred_element_type=jnp.float32)
     ).astype(jnp.bfloat16)
-    gathered = lax.all_gather(embedded, "tp", axis=1, tiled=True)
+    ring = [embedded]
+    for hop in range(7):
+        ring.append(lax.ppermute(ring[-1], "tp", [(dev, (dev + 1) % 8) for dev in range(8)]))
+    gathered = jnp.roll(
+        jnp.concatenate(ring[::-1], axis=1), (lax.axis_index("tp") + 1) * ring[0].shape[1], axis=1
+    )
     normed = normalize(gathered, norm_gain)
     projected = jnp.dot(
         normed,

time: 353 us -> 311 us (0.88); the launches traced: 353 us -> 306 us
  waiting for transfers between devices: 298 us -> 235 us
  starting transfers between devices: 14.3 us -> 28.4 us
    all_gather x1, waiting for transfers between devices: 85.4 us -> 0.02 us  [shards(): lax.all_gather(qkv_weight, 'req', axis=0, tiled=True)]
    ppermute x0 -> x7, waiting for transfers between devices: none -> 63 us  [shards(): lax.ppermute(ring[-1], 'tp', [(dev, (dev + 1) % 8) for dev in range(8)])]
    all_gather x1 -> x0, waiting for transfers between devices: 40 us -> none  [shards(): gathered = lax.all_gather(embedded, 'tp', axis=1, tiled=True)]
    ppermute x0 -> x7, starting transfers between devices: none -> 14.1 us  [shards(): lax.ppermute(ring[-1], 'tp', [(dev, (dev + 1) % 8) for dev in range(8)])]
  transfers between devices with their start and end apart: 5 -> 11, of which waited for: 5 -> 10; matrix products, arithmetic and copies ran while one was open for 3% -> 4% of each run, Pallas kernels for 0% -> 0%
where the time goes in v1:
time: 311 us; the launch traced here: 306 us
  waiting for transfers between devices  235 us (76%)
  starting transfers between devices  28.4 us (9%)
  between operations  15.5 us (5%)
  matrix products  13.2 us (4%)
  local copies, waits for them, and re-layouts  6.99 us (2%)
  other arithmetic  6.23 us (2%)
    all_gather x1, waiting for transfers between devices, shards(): lax.all_gather(out_weight, 'req', axis=1, tiled=True)  91.7 us
    psum x1, waiting for transfers between devices, shards(): lax.psum(partial_value.astype(jnp.bfloat16), 'tp').astype(jnp.float32)  72.7 us
    ppermute x7, waiting for transfers between devices, shards(): lax.ppermute(ring[-1], 'tp', [(dev, (dev + 1) % 8) for dev in range(8)])  63 us
    all_to_all x1, starting transfers between devices, shards(): lax.all_to_all(outgoing.reshape(requests, capacity, feature_width), 'req'...  14.2 us
    ppermute x7, starting transfers between devices, shards(): lax.ppermute(ring[-1], 'tp', [(dev, (dev + 1) % 8) for dev in range(8)])  14.1 us
    dot_general x1, matrix products, shards(): jnp.dot(normed, lax.all_gather(qkv_weight, 'req', axis=0, tiled=True), pr...  6.75 us
    all_to_all x1, waiting for transfers between devices, shards(): lax.all_to_all(outgoing.reshape(requests, capacity, feature_width), 'req'...  6.59 us
  transfers between devices with their start and end apart: 11, of which 10 were waited for; matrix products, arithmetic and copies ran while one was open for 4% of the time, Pallas kernels for 0%

profile of v1, /device:TPU:1, one launch (start us, length us, event | category | flops | bytes accessed | tf_op | source)
XLA Modules:
  0.0 305.6 jit_solution(2628359597963781023)
XLA Ops:
  6.6 0.7 all-gather.3.cloned.1.call-update
  7.3 0.0 all-reduce.2.cloned.1.call-start
  7.3 1.4 reshape.205
  8.7 0.6 reduce_sum.78
  9.3 91.7 %all-gather.3.cloned.1.call-done = bf16[512,4096]{0,1:T(8,128)(2,1)} async-done(((bf16[512,64]{0,1:T(8,128)(2,1)}), bf16[512,4096]{0,1:T(8,128)(2,1)}) %all-gather.3.cloned.1.call-update) | async-done | bytes 4194320 | tf_op jit(solution)/shard_map/all_gather | solution.py:78
  101.1 4.7 %convolution_convert_fusion = bf16[128,4096]{1,0:T(8,128)(2,1)} fusion(bf16[512,4096]{0,1:T(8,128)(2,1)} %all-gather.3.cloned.1.call-done, f32[128,512]{1,0:T(8,128)S(1)} %reduce_sum.78), kind=kOutput, calls=%fused_computation.5 | convolution fusion | flops 537526272 | bytes 5505024 | tf_op jit(solution)/shard_map/dot_general | solution.py:76
  105.8 0.0 all-gather.5.cloned.1.call-start
  105.8 0.7 all-gather.5.cloned.1.call-update
  106.5 0.1 select_reduce_fusion.1
  106.6 0.1 copy.16
  106.7 0.1 reduce-window.7
  106.8 0.1 reduce
  107.0 0.3 reshape.203
  107.3 0.6 reduce_sum.77
  107.9 0.1 convert_reduce_fusion
  108.0 0.7 fusion.39
  108.7 0.1 select_reduce_fusion
  108.8 72.7 %all-reduce.2.cloned.1.call-done = bf16[128,4096]{1,0:T(8,128)(2,1)} async-done(((bf16[128,4096]{1,0:T(8,128)(2,1)}), bf16[128,4096]{1,0:T(8,128)(2,1)}) %all-reduce.2.cloned.1.call-update) | async-done | bytes 1048592 | tf_op jit(solution)/shard_map/psum | solution.py:81
  181.5 1.1 convolution_convert_fusion.1
  182.6 0.7 reshape.199
  183.3 14.2 %all-to-all-start = ((bf16[64,2,512]{2,1,0:T(2,128)(2,1)}), bf16[64,2,512]{2,1,0:T(2,128)(2,1)S(1)}, u32[]{:S(2)}, u32[]{:S(2)}) async-start(bf16[64,2,512]{2,1,0:T(2,128)(2,1)} %reshape.199), calls=%async_computation | async-start | bytes 262144 | tf_op jit(solution)/shard_map/all_to_all | solution.py:101
  199.4 0.6 fusion.38
  200.0 1.2 fusion.31
  201.3 6.6 %all-to-all-done = bf16[64,2,512]{2,1,0:T(2,128)(2,1)S(1)} async-done(((bf16[64,2,512]{2,1,0:T(2,128)(2,1)}), bf16[64,2,512]{2,1,0:T(2,128)(2,1)S(1)}, u32[]{:S(2)}, u32[]{:S(2)}) %all-to-all-start) | async-done | bytes 131104 | tf_op jit(solution)/shard_map/all_to_all | solution.py:101
  207.9 0.1 reshape.200
  207.9 0.3 fusion.15
  208.2 0.3 fusion.8
  208.6 2.7 collective-permute-start
  211.3 10.8 %collective-permute-done = bf16[384,512]{1,0:T(8,128)(2,1)S(1)} collective-permute-done((bf16[384,512]{1,0:T(8,128)(2,1)S(1)}, bf16[384,512]{1,0:T(8,128)(2,1)S(1)}, u32[]{:S(2)}, u32[]{:S(2)}) %collective-permute-start) | collective-permute-done | bytes 393248 | tf_op jit(solution)/shard_map/ppermute | solution.py:135
  222.1 1.9 collective-permute-start.1
  224.0 10.7 %collective-permute-done.1 = bf16[384,512]{1,0:T(8,128)(2,1)S(1)} collective-permute-done((bf16[384,512]{1,0:T(8,128)(2,1)S(1)}, bf16[384,512]{1,0:T(8,128)(2,1)S(1)}, u32[]{:S(2)}, u32[]{:S(2)}) %collective-permute-start.1) | collective-permute-done | bytes 393248 | tf_op jit(solution)/shard_map/ppermute | solution.py:135
  234.7 1.9 collective-permute-start.2
  236.6 9.8 %collective-permute-done.2 = bf16[384,512]{1,0:T(8,128)(2,1)S(1)} collective-permute-done((bf16[384,512]{1,0:T(8,128)(2,1)S(1)}, bf16[384,512]{1,0:T(8,128)(2,1)S(1)}, u32[]{:S(2)}, u32[]{:S(2)}) %collective-permute-start.2) | collective-permute-done | bytes 393248 | tf_op jit(solution)/shard_map/ppermute | solution.py:135
  246.4 1.9 collective-permute-start.3
  248.3 9.0 %collective-permute-done.3 = bf16[384,512]{1,0:T(8,128)(2,1)S(1)} collective-permute-done((bf16[384,512]{1,0:T(8,128)(2,1)S(1)}, bf16[384,512]{1,0:T(8,128)(2,1)S(1)}, u32[]{:S(2)}, u32[]{:S(2)}) %collective-permute-start.3) | collective-permute-done | bytes 393248 | tf_op jit(solution)/shard_map/ppermute | solution.py:135
  257.4 1.9 collective-permute-start.4
  259.3 8.1 %collective-permute-done.4 = bf16[384,512]{1,0:T(8,128)(2,1)S(1)} collective-permute-done((bf16[384,512]{1,0:T(8,128)(2,1)S(1)}, bf16[384,512]{1,0:T(8,128)(2,1)S(1)}, u32[]{:S(2)}, u32[]{:S(2)}) %collective-permute-start.4) | collective-permute-done | bytes 393248 | tf_op jit(solution)/shard_map/ppermute | solution.py:135
  267.4 1.9 collective-permute-start.5
  269.3 7.8 %collective-permute-done.5 = bf16[384,512]{1,0:T(8,128)(2,1)S(1)} collective-permute-done((bf16[384,512]{1,0:T(8,128)(2,1)S(1)}, bf16[384,512]{1,0:T(8,128)(2,1)S(1)}, u32[]{:S(2)}, u32[]{:S(2)}) %collective-permute-start.5) | collective-permute-done | bytes 393248 | tf_op jit(solution)/shard_map/ppermute | solution.py:135
  277.1 1.9 collective-permute-start.6
  279.1 1.1 fusion.22
  280.1 6.7 %collective-permute-done.6 = bf16[384,512]{1,0:T(8,128)(2,1)S(1)} collective-permute-done((bf16[384,512]{1,0:T(8,128)(2,1)S(1)}, bf16[384,512]{1,0:T(8,128)(2,1)S(1)}, u32[]{:S(2)}, u32[]{:S(2)}) %collective-permute-start.6) | collective-permute-done | bytes 393248 | tf_op jit(solution)/shard_map/ppermute | solution.py:135
  287.6 2.7 copy-done.1
  290.3 0.7 fusion
  291.0 6.7 %fusion.3 = f32[384,768]{0,1:T(8,128)S(1)} fusion(bf16[4096,768]{1,0:T(8,128)(2,1)} %all-gather.5.cloned.1.call-done, f32[4096]{0:T(1024)S(1)} %copy-done.5, f32[384]{0:T(512)S(1)} %add_rsqrt_fusion, bf16[384,8192]{1,0:T(8,128)(2,1)} %copy-done.1, s32[]{:T(128)S(6)} %select_n.71), kind=kOutput, calls=%fused_computation.6 | convolution fusion | flops 2422210560 | bytes 10634756 | tf_op jit(solution)/shard_map/dot_general | solution.py:140
  297.8 0.1 subtract_convert_fusion
  297.9 0.1 pad_maximum_fusion
  298.0 1.1 copy.18
  (41 shorter events, 0.8 us)
Async XLA Ops:
  6.5 201.7 %copy-start = (bf16[1,256,512]{2,1,0:T(8,128)(2,1)S(1)}, bf16[1,256,512]{2,1,0:T(8,128)(2,1)}, u32[]{:S(2)}) copy-start(bf16[1,256,512]{2,1,0:T(8,128)(2,1)} %param.15) | copy-start | bytes 786436
  6.5 100.0 %copy-start.6 = (s32[128,2]{0,1:T(2,128)S(1)}, s32[128,2]{0,1:T(2,128)}, u32[]{:S(2)}) copy-start(s32[128,2]{0,1:T(2,128)} %param.18) | copy-start | bytes 3076
  6.5 100.0 %copy-start.7 = (s32[128]{0:T(128)S(1)}, s32[128]{0:T(128)}, u32[]{:S(2)}) copy-start(s32[128]{0:T(128)} %param.19) | copy-start | bytes 1540
  6.5 100.4 %copy-start.2 = (bf16[512,512]{1,0:T(8,128)(2,1)S(1)}, bf16[512,512]{1,0:T(8,128)(2,1)}, u32[]{:S(2)}) copy-start(bf16[512,512]{1,0:T(8,128)(2,1)} %param.12) | copy-start | bytes 1572868
  6.5 94.5 %all-gather.3.cloned.1.call-start = ((), (), s32[]{:S(2)}) async-start(), calls=%async_computation.1 | async-start | bytes 4259840 | tf_op jit(solution)/shard_map/all_gather | solution.py:78
  7.3 174.2 %copy-start.4 = (f32[512]{0:T(512)S(1)}, f32[512]{0:T(512)}, u32[]{:S(2)}) copy-start(f32[512]{0:T(512)} %param.14) | copy-start | bytes 6148
  7.3 174.2 %all-reduce.2.cloned.1.call-start = ((), (), s32[]{:S(2)}) async-start(), calls=%async_computation.2 | async-start | bytes 2097152 | tf_op jit(solution)/shard_map/psum | solution.py:81
  105.8 185.2 %all-gather.5.cloned.1.call-start = ((), (), s32[]{:S(2)}) async-start(), calls=%async_computation.3 | async-start | bytes 6389760 | tf_op jit(solution)/shard_map/all_gather | solution.py:142
  183.3 24.5 %all-to-all-start = ((bf16[64,2,512]{2,1,0:T(2,128)(2,1)}), bf16[64,2,512]{2,1,0:T(2,128)(2,1)S(1)}, u32[]{:S(2)}, u32[]{:S(2)}) async-start(bf16[64,2,512]{2,1,0:T(2,128)(2,1)} %reshape.199), calls=%async_computation | async-start | bytes 262144 | tf_op jit(solution)/shard_map/all_to_all | solution.py:101
  208.6 13.5 %collective-permute-start = (bf16[384,512]{1,0:T(8,128)(2,1)S(1)}, bf16[384,512]{1,0:T(8,128)(2,1)S(1)}, u32[]{:S(2)}, u32[]{:S(2)}) collective-permute-start(bf16[384,512]{1,0:T(8,128)(2,1)S(1)} %fusion.8), channel_id=1, source_target_pairs={{0,1},{1,2},{2,3},{3,4},{4,5},{5,6},{6,7},{7,0},{8,9},{9,10},{10,1... | collective-permute-start | bytes 1179656 | tf_op jit(solution)/shard_map/ppermute | solution.py:135
  222.1 12.6 %collective-permute-start.1 = (bf16[384,512]{1,0:T(8,128)(2,1)S(1)}, bf16[384,512]{1,0:T(8,128)(2,1)S(1)}, u32[]{:S(2)}, u32[]{:S(2)}) collective-permute-start(bf16[384,512]{1,0:T(8,128)(2,1)S(1)} %collective-permute-done), channel_id=1, source_target_pairs={{0,1},{1,2},{2,3},{3,4},{4,5},{5,6},{6,7},{7,0},{8,9},{9,10},{10,1... | collective-permute-start | bytes 1179656 | tf_op jit(solution)/shard_map/ppermute | solution.py:135
  234.7 11.8 %collective-permute-start.2 = (bf16[384,512]{1,0:T(8,128)(2,1)S(1)}, bf16[384,512]{1,0:T(8,128)(2,1)S(1)}, u32[]{:S(2)}, u32[]{:S(2)}) collective-permute-start(bf16[384,512]{1,0:T(8,128)(2,1)S(1)} %collective-permute-done.1), channel_id=1, source_target_pairs={{0,1},{1,2},{2,3},{3,4},{4,5},{5,6},{6,7},{7,0},{8,9},{9,10},{10,1... | collective-permute-start | bytes 1179656 | tf_op jit(solution)/shard_map/ppermute | solution.py:135
  246.4 10.9 %collective-permute-start.3 = (bf16[384,512]{1,0:T(8,128)(2,1)S(1)}, bf16[384,512]{1,0:T(8,128)(2,1)S(1)}, u32[]{:S(2)}, u32[]{:S(2)}) collective-permute-start(bf16[384,512]{1,0:T(8,128)(2,1)S(1)} %collective-permute-done.2), channel_id=1, source_target_pairs={{0,1},{1,2},{2,3},{3,4},{4,5},{5,6},{6,7},{7,0},{8,9},{9,10},{10,1... | collective-permute-start | bytes 1179656 | tf_op jit(solution)/shard_map/ppermute | solution.py:135
  257.4 10.0 %collective-permute-start.4 = (bf16[384,512]{1,0:T(8,128)(2,1)S(1)}, bf16[384,512]{1,0:T(8,128)(2,1)S(1)}, u32[]{:S(2)}, u32[]{:S(2)}) collective-permute-start(bf16[384,512]{1,0:T(8,128)(2,1)S(1)} %collective-permute-done.3), channel_id=1, source_target_pairs={{0,1},{1,2},{2,3},{3,4},{4,5},{5,6},{6,7},{7,0},{8,9},{9,10},{10,1... | collective-permute-start | bytes 1179656 | tf_op jit(solution)/shard_map/ppermute | solution.py:135
  267.4 9.7 %collective-permute-start.5 = (bf16[384,512]{1,0:T(8,128)(2,1)S(1)}, bf16[384,512]{1,0:T(8,128)(2,1)S(1)}, u32[]{:S(2)}, u32[]{:S(2)}) collective-permute-start(bf16[384,512]{1,0:T(8,128)(2,1)S(1)} %collective-permute-done.4), channel_id=1, source_target_pairs={{0,1},{1,2},{2,3},{3,4},{4,5},{5,6},{6,7},{7,0},{8,9},{9,10},{10,1... | collective-permute-start | bytes 1179656 | tf_op jit(solution)/shard_map/ppermute | solution.py:135
  277.1 9.7 %collective-permute-start.6 = (bf16[384,512]{1,0:T(8,128)(2,1)S(1)}, bf16[384,512]{1,0:T(8,128)(2,1)S(1)}, u32[]{:S(2)}, u32[]{:S(2)}) collective-permute-start(bf16[384,512]{1,0:T(8,128)(2,1)S(1)} %collective-permute-done.5), channel_id=1, source_target_pairs={{0,1},{1,2},{2,3},{3,4},{4,5},{5,6},{6,7},{7,0},{8,9},{9,10},{10,1... | collective-permute-start | bytes 1179656 | tf_op jit(solution)/shard_map/ppermute | solution.py:135
  287.0 4.0 %copy-start.5 = (f32[4096]{0:T(1024)S(1)}, f32[4096]{0:T(1024)}, u32[]{:S(2)}) copy-start(f32[4096]{0:T(1024)} %param.20) | copy-start | bytes 49156
  287.6 2.7 copy-start.1
  291.0 6.8 %copy-start.3 = (f32[384,64]{0,1:T(8,128)S(1)}, f32[384,64]{0,1:T(8,128)}, u32[]{:S(2)}) copy-start(f32[384,64]{0,1:T(8,128)} %get-tuple-element.12) | copy-start | bytes 294916
Sparse Core Ops, SparseCore 0:
  10.7 90.2 all-gather.2
  105.9 75.5 all-reduce.1
  184.8 88.4 all-gather.4
